TPU v7x, 256 devices: a whole 4x4x8 slice. The times are simulated.
256 devices in a mesh: seq: 64 (over z, y, core), mp: 4 (over x).
Axes of the slice: x: 4, y: 4, z: 8, core: 2. Of those that a mesh axis runs over, the one named last changes fastest.
Arguments:
- patches: bfloat16 [262144, 1280], P('seq'), may hold values from -2 to 2
- w_qkv: bfloat16 [1280, 3840], P('seq', 'mp'), as said below
- w_out: bfloat16 [1280, 1280], P('mp', 'seq'), may hold values from -0.15625 to 0.15625
- page_rows: int32 [64], replicated, may hold values from 32 to 64, as said below
- page_cols: int32 [64], replicated, may hold values from 32 to 64, as said below
- window_slot: int32 [64, 64], replicated, may hold values from 0 to 63, each once within a row
Outputs:
- blocks: bfloat16 [262144, 1280], P('seq', 'mp')
Inputs may be any that keep to these rules, and one draw needn't show every extreme that they name: `page_rows`: page heights, multiples of 16; some page has the largest. `page_cols`: page widths, multiples of 16; some page has the largest. `window_slot`: each row is a permutation. `w_qkv`: entries of order at most 5.5 / sqrt(1280).
All inputs are finite; a program needn't handle non-finite values.
Results may differ from a plain program's by a relative error of at most 0.012.
Values may be sent and summed in bfloat16 or wider, within the bound.
No kernel may reach another device: no remote copies, remote signals or barrier semaphores. Data moves between devices by JAX's collectives and lax.ppermute only.
A program may use at most 192 MiB of HBM per device.

v0:
```python
import jax
import jax.numpy as jnp
from jax import lax
from jax.sharding import PartitionSpec as P

HD = 80
WS = 8
QUARTERS = 4
EPSILON = 1e-06


def angle_tables(row_place, column_place, head_size):
    quarter = head_size // 4
    frequency = 1.0 / 10000.0 ** (jnp.arange(quarter, dtype=jnp.float32) * 2.0 / (head_size // 2))
    angles = jnp.concatenate(
        [
            row_place[..., None].astype(jnp.float32) * frequency,
            column_place[..., None].astype(jnp.float32) * frequency,
        ],
        axis=-1,
    )
    angles = jnp.concatenate([angles, angles], axis=-1)
    return (jnp.cos(angles), jnp.sin(angles))


def slot_positions(page_widths, slot_table, slot_numbers, window_side):
    matches = slot_table[:, :, None] == slot_numbers[None, None, :]
    ordinal = jnp.arange(slot_table.shape[1], dtype=jnp.int32)
    window = jnp.sum(jnp.where(matches, ordinal[None, :, None], 0), axis=1)
    across = page_widths // window_side
    window_row = window // across[:, None]
    window_column = window % across[:, None]
    unit_side = window_side // 2
    position = jnp.arange(window_side * window_side, dtype=jnp.int32)
    merge_unit = position // 4
    corner = position % 4
    inner_row = merge_unit // unit_side * 2 + corner // 2
    inner_column = merge_unit % unit_side * 2 + corner % 2
    row_place = window_row[:, :, None] * window_side + inner_row
    column_place = window_column[:, :, None] * window_side + inner_column
    return (row_place, column_place)


def block_sources(height, page_width, slot_row, block_count):
    across = page_width // WS
    block = jnp.arange(block_count, dtype=jnp.int32)
    band = block // across
    column = block % across
    window_row = band // QUARTERS
    quarter = band % QUARTERS
    live = window_row < height // WS
    window = jnp.where(live, window_row * across + column, 0)
    ordinal = jnp.arange(slot_row.shape[0], dtype=jnp.int32)
    slot = jnp.sum(jnp.where(window[:, None] == ordinal[None, :], slot_row[None, :], 0), axis=1)
    return (slot * QUARTERS + quarter, live)


def normalize(block_in):
    values = block_in.astype(jnp.float32)
    factor = lax.rsqrt(jnp.mean(values * values, axis=-1, keepdims=True) + EPSILON)
    return (values * factor).astype(jnp.bfloat16)


def rotated_columns(weight):
    half = weight.shape[-1] // 2
    return jnp.concatenate([-weight[..., half:], weight[..., :half]], axis=-1)


def local(patches, w_qkv, w_out, page_rows, page_cols, window_slot):
    seq_index = lax.axis_index("seq")
    seq_count = lax.axis_size("seq")
    mp_index = lax.axis_index("mp")
    page_count = window_slot.shape[0]
    slot_count = window_slot.shape[1]
    slots_held = slot_count // seq_count
    window_tokens = WS * WS
    quarter_tokens = window_tokens // QUARTERS
    model_width = patches.shape[1]
    windows = patches.shape[0] // window_tokens
    own_rows = w_qkv.shape[0]
    heads = w_qkv.shape[1] // (3 * HD)
    qkv = w_qkv.reshape(own_rows, heads, 3, HD)
    w_q = qkv[:, :, 0]
    w_k = qkv[:, :, 1]
    fused_rows = jnp.concatenate(
        [
            w_q.reshape(own_rows, heads * HD),
            w_k.reshape(own_rows, heads * HD),
            rotated_columns(w_q).reshape(own_rows, heads * HD),
            rotated_columns(w_k).reshape(own_rows, heads * HD),
            qkv[:, :, 2].reshape(own_rows, heads * HD),
            w_out.T,
        ],
        axis=1,
    )
    joined = lax.all_gather(fused_rows, "seq", axis=0, tiled=True)
    fused = joined[:, : 5 * heads * HD]
    out_rows_t = joined[:, 5 * heads * HD :]
    out_full_t = lax.all_gather(out_rows_t, "mp", axis=1, tiled=True)
    slot_numbers = seq_index * slots_held + jnp.arange(slots_held, dtype=jnp.int32)
    row_place, column_place = slot_positions(page_cols, window_slot, slot_numbers, WS)
    cosine, sine = angle_tables(
        row_place.reshape(-1, window_tokens), column_place.reshape(-1, window_tokens), HD
    )
    cosine = jnp.tile(cosine.reshape(-1, HD), (1, 2 * heads))
    sine = jnp.tile(sine.reshape(-1, HD), (1, 2 * heads))
    normed = normalize(patches)
    projected = jnp.dot(normed, fused, preferred_element_type=jnp.float32)
    width = heads * HD
    turned = projected[:, : 2 * width] * cosine + projected[:, 2 * width : 4 * width] * sine
    turned = turned.astype(jnp.bfloat16).reshape(windows, window_tokens, 2 * width)
    queries = turned[:, :, :width]
    key_block = turned[:, :, width:]
    values = projected[:, 4 * width :].astype(jnp.bfloat16).reshape(windows, window_tokens, width)
    lane_head = jnp.arange(width, dtype=jnp.int32) // HD
    scale = 1.0 / HD**0.5
    mixed = jnp.zeros((windows, window_tokens, width), jnp.float32)
    for head in range(heads):
        mask = lane_head == head
        picked = jnp.where(mask, queries, jnp.zeros_like(queries))
        scores = (
            jnp.einsum("wqd,wkd->wqk", picked, key_block, preferred_element_type=jnp.float32)
            * scale
        )
        row_max = jnp.max(scores, axis=-1, keepdims=True)
        lifted = jnp.exp(scores - row_max)
        weights = (lifted / jnp.sum(lifted, axis=-1, keepdims=True)).astype(jnp.bfloat16)
        own_values = jnp.where(mask, values, jnp.zeros_like(values))
        mixed = mixed + jnp.einsum(
            "wqk,wkd->wqd", weights, own_values, preferred_element_type=jnp.float32
        )
    mixed = mixed.astype(jnp.bfloat16)
    spread = mixed.reshape(windows, QUARTERS, quarter_tokens, width)
    gathered = lax.all_to_all(spread, "mp", split_axis=1, concat_axis=1, tiled=True)
    out_grouped = out_full_t.reshape(model_width, QUARTERS, width)
    branch = lax.dot_general(
        gathered, out_grouped, (((1, 3), (1, 2)), ((), ())), preferred_element_type=jnp.float32
    )
    branch = branch.reshape(windows * quarter_tokens, model_width)
    residual = patches.reshape(windows, QUARTERS, quarter_tokens, model_width)
    residual = lax.dynamic_index_in_dim(residual, mp_index, 1, keepdims=False)
    residual = residual.reshape(windows * quarter_tokens, model_width).astype(jnp.float32)
    block_out = (residual + branch).astype(jnp.bfloat16)
    share_width = model_width // QUARTERS
    sectioned = block_out.reshape(page_count, quarter_tokens, QUARTERS, share_width)
    sectioned = jnp.transpose(sectioned, (0, 2, 1, 3)).reshape(
        page_count * QUARTERS, quarter_tokens, share_width
    )
    landed = lax.all_to_all(sectioned, ("seq", "mp"), split_axis=0, concat_axis=0, tiled=True)
    own_pages = page_count // seq_count
    first_page = seq_index * own_pages
    heights = lax.dynamic_slice_in_dim(page_rows, first_page, own_pages, 0)
    widths = lax.dynamic_slice_in_dim(page_cols, first_page, own_pages, 0)
    slot_rows = lax.dynamic_slice_in_dim(window_slot, first_page, own_pages, 0)
    block_count = slot_count * QUARTERS // own_pages
    landed = landed.reshape(own_pages, block_count, quarter_tokens, share_width)

    def regroup(received, height, page_width, slot_row):
        source, live = block_sources(height, page_width, slot_row, block_count)
        picked = jnp.take(received, source, axis=0)
        return jnp.where(live[:, None, None], picked, jnp.zeros_like(picked))

    merged = jax.vmap(regroup)(landed, heights, widths, slot_rows)
    return merged.reshape(-1, share_width)


def solution(mesh):
    return jax.shard_map(
        local,
        mesh=mesh,
        in_specs=(P("seq", None), P("seq", "mp"), P("mp", "seq"), P(), P(), P()),
        out_specs=P("seq", "mp"),
        check_vma=False,
    )
```

profile of v0, /device:TPU:1, one launch (start us, length us, event | category | flops | bytes accessed | tf_op | source)
XLA Modules:
  0.0 355.9 jit_solution(10992189034661572990)
XLA Ops:
  8.7 1.5 concatenate.24
  12.5 6.1 %fusion.4 = f32[4096]{0:T(1024)S(1)} fusion(bf16[4096,1280]{1,0:T(8,128)(2,1)} %param.6), kind=kLoop, calls=%fused_computation.7 | loop fusion | flops 15724544 | bytes 10502144 | tf_op jit(solution)/shard_map/reduce_sum | solution.py:60
  18.7 4.8 %fusion.69 = (f32[4096,80]{0,1:T(8,128)S(1)}, f32[4096,80]{0,1:T(8,128)S(1)}) fusion(f32[4096,20]{0,1:T(8,128)S(1)} %get-tuple-element.19, f32[4096,20]{0,1:T(8,128)S(1)} %get-tuple-element.18), kind=kLoop, calls=%fused_computation.88 | loop fusion | flops 983040 | bytes 3276800 | tf_op jit(solution)/shard_map/cos | solution.py:23
  23.5 71.3 %all-gather.6.cloned.1.call-done = bf16[64,20,1920]{2,1,0:T(8,128)(2,1)} async-done(((bf16[1,20,1920]{2,1,0:T(8,128)(2,1)}), bf16[64,20,1920]{2,1,0:T(8,128)(2,1)}) %all-gather.6.cloned.1.call-update) | async-done | bytes 4915216 | tf_op jit(solution)/shard_map/all_gather | solution.py:96
  94.8 7.5 %reshape.662 = bf16[1280,1920]{1,0:T(8,128)(2,1)} reshape(bf16[64,20,1920]{2,1,0:T(8,128)(2,1)} %all-gather.6.cloned.1.call-done) | data formatting | bytes 9830400
  102.3 2.6 slice.72
  104.9 2.2 copy.67
  107.2 23.8 %fusion.6 = f32[4096,1600]{0,1:T(8,128)} fusion(bf16[4096,1280]{1,0:T(8,128)(2,1)} %param.6, f32[4096]{0:T(1024)S(1)} %add_rsqrt_fusion, bf16[1280,1920]{1,0:T(8,128)(2,1)} %reshape.662), kind=kOutput, calls=%fused_computation.9 | convolution fusion | flops 16792944640 | bytes 40976384 | tf_op jit(solution)/shard_map/dot_general | solution.py:108
  131.0 4.4 %slice.125 = bf16[4096,320]{0,1:T(8,128)(2,1)} slice(f32[4096,1600]{0,1:T(8,128)} %fusion.6), slice={[0:4096], [1280:1600]} | slice | bytes 5242880 | tf_op jit(solution)/shard_map/slice | solution.py:114
  135.4 10.4 %fusion.9 = bf16[4096,640]{0,1:T(8,128)(2,1)} fusion(f32[4096,1600]{0,1:T(8,128)} %fusion.6, f32[4096,80]{0,1:T(8,128)S(1)} %get-tuple-element.11, f32[4096,80]{0,1:T(8,128)S(1)} %get-tuple-element.10), kind=kLoop, calls=%fused_computation.12 | loop fusion | flops 10485760 | bytes 28835840 | tf_op jit(solution)/shard_map/convert_element_type | solution.py:111
  145.8 7.9 %copy.60 = bf16[4096,640]{1,0:T(8,128)(2,1)} copy(bf16[4096,640]{0,1:T(8,128)(2,1)} %fusion.9) | data formatting | bytes 10485760 | tf_op jit(solution)/shard_map/convert_element_type | solution.py:111
  153.7 3.5 copy.61
  157.2 5.4 %fusion.20 = f32[64,64,64]{1,2,0:T(8,128)S(1)} fusion(pred[320]{0:T(512)(128)(4,1)S(1)} %broadcast_compare_fusion.1, bf16[64,64,640]{2,1,0:T(8,128)(2,1)} %bitcast.54), kind=kOutput, calls=%fused_computation.28 | convolution fusion | flops 169082880 | bytes 7340352 | tf_op jit(solution)/shard_map/wqd,wkd->wqk/dot_general | solution.py:122
  164.0 1.4 fusion.16
  165.4 1.4 fusion.28
  166.7 1.4 fusion.24
  170.1 5.4 %fusion.22 = f32[64,64,320]{2,1,0:T(8,128)} fusion(bf16[64,64,320]{2,1,0:T(8,128)(2,1)S(1)} %bitcast.50, pred[320]{0:T(512)(128)(4,1)S(1)} %broadcast_compare_fusion.3, f32[64,64]{1,0:T(8,128)S(1)} %fusion.127, f32[64,64,64]{1,2,0:T(8,128)} %copy-done.7), kind=kOutput, calls=%fused_computation.30 | convolution fusion | flops 170135616 | bytes 8929600 | tf_op jit(solution)/shard_map/wqk,wkd->wqd/dot_general | solution.py:129
  175.5 5.4 %fusion.14 = f32[64,64,320]{2,1,0:T(8,128)} fusion(bf16[64,64,320]{2,1,0:T(8,128)(2,1)S(1)} %bitcast.51, pred[320]{0:T(512)(128)(4,1)S(1)} %broadcast_compare_fusion, f32[64,64]{1,0:T(8,128)S(1)} %fusion.125, f32[64,64,64]{1,2,0:T(8,128)} %copy-done.6), kind=kOutput, calls=%fused_computation.22 | convolution fusion | flops 170135616 | bytes 8929600 | tf_op jit(solution)/shard_map/wqk,wkd->wqd/dot_general | solution.py:129
  180.9 5.3 %fusion.18 = f32[64,64,320]{2,1,0:T(8,128)} fusion(bf16[64,64,320]{2,1,0:T(8,128)(2,1)S(1)} %bitcast.52, pred[320]{0:T(512)(128)(4,1)S(1)} %broadcast_compare_fusion.1, f32[64,64]{1,0:T(8,128)S(1)} %fusion.126, f32[64,64,64]{1,2,0:T(8,128)} %copy-done.5), kind=kOutput, calls=%fused_computation.26 | convolution fusion | flops 170135616 | bytes 8929600 | tf_op jit(solution)/shard_map/wqk,wkd->wqd/dot_general | solution.py:129
  186.2 9.9 %add_convert_fusion = bf16[64,64,320]{2,1,0:T(8,128)(2,1)S(1)} fusion(f32[64,64,320]{2,1,0:T(8,128)} %fusion.14, f32[64,64,320]{2,1,0:T(8,128)} %fusion.18, f32[64,64,320]{2,1,0:T(8,128)} %fusion.22, bf16[64,64,320]{2,1,0:T(8,128)(2,1)} %bitcast.53, pred[320]{0:T(512)(128)(4,1)S(1)} %broadcast_compare_fusion.2, f32[64,64]{1,0:T(8,128)S(1)} %fusion.128, ...), kind=kOutput, calls=%fused_computation.15 | convolution fusion | flops 175378496 | bytes 22036800 | tf_op jit(solution)/shard_map/wqk,wkd->wqd/dot_general | solution.py:129
  196.1 2.0 copy.66
  198.1 3.9 %all-to-all-start = ((bf16[64,4,16,320]{3,2,0,1:T(8,128)(2,1)}), bf16[64,4,16,320]{3,2,0,1:T(8,128)(2,1)S(1)}, u32[]{:S(2)}, u32[]{:S(2)}) async-start(bf16[64,4,16,320]{3,2,0,1:T(8,128)(2,1)} %copy.66), calls=%async_computation | async-start | bytes 6291456 | tf_op jit(solution)/shard_map/all_to_all | solution.py:134
  201.9 3.4 constant_dynamic-slice_fusion
  205.4 33.7 %all-to-all-done = bf16[64,4,16,320]{3,2,0,1:T(8,128)(2,1)S(1)} async-done(((bf16[64,4,16,320]{3,2,0,1:T(8,128)(2,1)}), bf16[64,4,16,320]{3,2,0,1:T(8,128)(2,1)S(1)}, u32[]{:S(2)}, u32[]{:S(2)}) %all-to-all-start) | async-done | bytes 2621472 | tf_op jit(solution)/shard_map/all_to_all | solution.py:134
  239.0 7.3 %fusion.11 = bf16[1024,1280]{1,0:T(8,128)(2,1)} fusion(bf16[1024,1280]{1,0:T(8,128)(2,1)} %bitcast.59, bf16[1024,4,320]{2,0,1:T(8,128)(2,1)S(1)} %bitcast.58, bf16[1280,4,320]{0,2,1:T(8,128)(2,1)} %bitcast.63), kind=kOutput, calls=%fused_computation.18 | convolution fusion | flops 3359375360 | bytes 11141120 | tf_op jit(solution)/shard_map/dot_general | solution.py:136
  246.3 6.1 %reshape.648 = bf16[64,16,4,320]{3,2,1,0:T(4,128)(2,1)S(1)} reshape(bf16[1024,1280]{1,0:T(8,128)(2,1)} %fusion.11) | data formatting | bytes 5242880 | tf_op jit(solution)/shard_map/reshape | solution.py:145
  252.4 2.4 copy.69
  254.8 7.8 %all-to-all-start.1 = ((bf16[256,16,320]{2,1,0:T(8,128)(2,1)}), bf16[256,16,320]{2,1,0:T(8,128)(2,1)S(1)}, u32[]{:S(2)}, u32[]{:S(2)}) async-start(bf16[256,16,320]{2,1,0:T(8,128)(2,1)} %bitcast.48), calls=%async_computation.1 | async-start | bytes 6291456 | tf_op jit(solution)/shard_map/all_to_all | solution.py:149
  270.6 67.9 %all-to-all-done.1 = bf16[256,16,320]{2,1,0:T(8,128)(2,1)S(1)} async-done(((bf16[256,16,320]{2,1,0:T(8,128)(2,1)}), bf16[256,16,320]{2,1,0:T(8,128)(2,1)S(1)}, u32[]{:S(2)}, u32[]{:S(2)}) %all-to-all-start.1) | async-done | bytes 2621472 | tf_op jit(solution)/shard_map/all_to_all | solution.py:149
  338.6 2.7 gather_fusion
  341.3 5.0 %fusion.13 = bf16[4096,320]{1,0:T(8,128)(2,1)S(1)} fusion(bf16[256,16,320]{2,1,0:T(8,128)(2,1)} %gather_fusion, pred[4096]{0:T(1024)(128)(4,1)S(1)} %broadcast_in_dim.141, pred[4096]{0:T(1024)(128)(4,1)S(1)} %broadcast_in_dim.135), kind=kLoop, calls=%fused_computation.21 | loop fusion | flops 2621440 | bytes 5251072 | tf_op jit(solution)/shard_map/vmap(jit(_where))/select_n | solution.py:161
  346.3 2.7 copy.70
  (66 shorter events, 10.7 us)
Async XLA Ops:
  6.5 88.3 %all-gather.6.cloned.1.call-start = ((), (), s32[]{:S(2)}) async-start(), calls=%async_computation.3 | async-start | bytes 5990400 | tf_op jit(solution)/shard_map/all_gather | solution.py:96
  10.2 228.8 %all-gather.4.cloned.1.call-start = ((), (), s32[]{:S(2)}) async-start(), calls=%async_computation.2 | async-start | bytes 4096000 | tf_op jit(solution)/shard_map/all_gather | solution.py:99
  157.2 23.6 %copy-start = (bf16[4096,320]{1,0:T(8,128)(2,1)}, bf16[4096,320]{1,0:T(8,128)(2,1)S(1)}, u32[]{:S(2)}) copy-start(bf16[4096,320]{1,0:T(8,128)(2,1)S(1)} %copy.61) | copy-start | bytes 7864324
  157.2 6.7 %copy-start.1 = (bf16[4096,640]{1,0:T(8,128)(2,1)S(1)}, bf16[4096,640]{1,0:T(8,128)(2,1)}, u32[]{:S(2)}) copy-start(bf16[4096,640]{1,0:T(8,128)(2,1)} %copy.60) | copy-start | bytes 15728644
  162.6 1.4 copy-start.5
  165.3 2.8 copy-start.6
  166.7 2.7 copy-start.2
  168.1 2.0 copy-start.7
  198.1 41.0 %all-to-all-start = ((bf16[64,4,16,320]{3,2,0,1:T(8,128)(2,1)}), bf16[64,4,16,320]{3,2,0,1:T(8,128)(2,1)S(1)}, u32[]{:S(2)}, u32[]{:S(2)}) async-start(bf16[64,4,16,320]{3,2,0,1:T(8,128)(2,1)} %copy.66), calls=%async_computation | async-start | bytes 6291456 | tf_op jit(solution)/shard_map/all_to_all | solution.py:134
  254.8 7.8 %copy-start.3 = (s32[64]{0:T(128)S(1)}, s32[64]{0:T(128)}, u32[]{:S(2)}) copy-start(s32[64]{0:T(128)} %param.10) | copy-start | bytes 772
  254.8 11.0 %copy-start.4 = (s32[64]{0:T(128)S(1)}, s32[64]{0:T(128)}, u32[]{:S(2)}) copy-start(s32[64]{0:T(128)} %param.9) | copy-start | bytes 772
  254.8 83.8 %all-to-all-start.1 = ((bf16[256,16,320]{2,1,0:T(8,128)(2,1)}), bf16[256,16,320]{2,1,0:T(8,128)(2,1)S(1)}, u32[]{:S(2)}, u32[]{:S(2)}) async-start(bf16[256,16,320]{2,1,0:T(8,128)(2,1)} %bitcast.48), calls=%async_computation.1 | async-start | bytes 6291456 | tf_op jit(solution)/shard_map/all_to_all | solution.py:149
Sparse Core Ops, SparseCore 0:
  10.4 84.3 all-gather.5
  107.3 39.4 all-gather.3
where the time goes:
time: 357 us; the launch traced here: 356 us
  waiting for transfers between devices  173 us (48%)
  matrix products  66.5 us (19%)
  local copies, waits for them, and re-layouts  54 us (15%)
  other arithmetic  31.8 us (9%)
  between operations  18.9 us (5%)
  starting transfers between devices  11.7 us (3%)
    all_gather x1, waiting for transfers between devices, local(): joined = lax.all_gather(fused_rows, 'seq', axis=0, tiled=True)  71.3 us
    all_to_all x1, waiting for transfers between devices, local(): lax.all_to_all(sectioned, ('seq', 'mp'), split_axis=0, concat_axis=0, til...  67.9 us
    all_to_all x1, waiting for transfers between devices, local(): lax.all_to_all(spread, 'mp', split_axis=1, concat_axis=1, tiled=True)  33.7 us
    dot_general x4, matrix products, local(): jnp.einsum('wqk,wkd->wqd', weights, own_values, preferred_element_type=jn...  26 us
    dot_general x1, matrix products, local(): projected = jnp.dot(normed, fused, preferred_element_type=jnp.float32)  23.8 us
    convert_element_type x1, other arithmetic, local(): turned.astype(jnp.bfloat16).reshape(windows, window_tokens, 2 * width)  10.4 us
    dot_general x4, matrix products, local(): jnp.einsum('wqd,wkd->wqk', picked, key_block, preferred_element_type=jnp....  9.45 us
    reshape x2, local copies, waits for them, and re-layouts, local(): block_out.reshape(page_count, quarter_tokens, QUARTERS, share_width)  8.5 us
  transfers between devices with their start and end apart: 4, of which 3 were waited for; matrix products, arithmetic and copies ran while one was open for 31% of the time, Pallas kernels for 0%

commit v1 on v0

--- a/solution.py
+++ b/solution.py
@@ -93,7 +93,9 @@
         ],
         axis=1,
     )
-    joined = lax.all_gather(fused_rows, "seq", axis=0, tiled=True)
+    joined = jnp.concatenate(
+        lax.all_to_all(jnp.stack([fused_rows] * lax.axis_size("seq")), "seq", 0, 0), axis=0
+    )
     fused = joined[:, : 5 * heads * HD]
     out_rows_t = joined[:, 5 * heads * HD :]
     out_full_t = lax.all_gather(out_rows_t, "mp", axis=1, tiled=True)

time: 357 us -> 420 us (1.18)
  waiting for transfers between devices: 173 us -> 218 us
  starting transfers between devices: 11.7 us -> 29.3 us
    all_to_all x0 -> x1, waiting for transfers between devices: none -> 118 us  [local(): lax.all_to_all(jnp.stack([fused_rows] * lax.axis_size('seq')), 'seq', 0, 0)]
    all_gather x1 -> x0, waiting for transfers between devices: 71.3 us -> none  [local(): joined = lax.all_gather(fused_rows, 'seq', axis=0, tiled=True)]
    all_to_all x0 -> x1, starting transfers between devices: none -> 13.4 us  [local(): lax.all_to_all(jnp.stack([fused_rows] * lax.axis_size('seq')), 'seq', 0, 0)]
    reshape x0 -> x1, local copies, waits for them, and re-layouts: none -> 7.54 us  [local(): jnp.concatenate(lax.all_to_all(jnp.stack([fused_rows] * lax.axis_size('se...]
    unnamed x18 -> x19, local copies, waits for them, and re-layouts: 8.29 us -> 0.76 us
  transfers between devices with their start and end apart: 4 -> 4, of which waited for: 3 -> 3; matrix products, arithmetic and copies ran while one was open for 31% -> 26% of each run, Pallas kernels for 0% -> 0%
where the time goes in v1:
time: 420 us; the launch traced here: 419 us
  waiting for transfers between devices  218 us (52%)
  matrix products  66.6 us (16%)
  local copies, waits for them, and re-layouts  55.7 us (13%)
  other arithmetic  30.5 us (7%)
  starting transfers between devices  29.3 us (7%)
  between operations  18.9 us (4%)
    all_to_all x1, waiting for transfers between devices, local(): lax.all_to_all(jnp.stack([fused_rows] * lax.axis_size('seq')), 'seq', 0, 0)  118 us
    all_to_all x1, waiting for transfers between devices, local(): lax.all_to_all(sectioned, ('seq', 'mp'), split_axis=0, concat_axis=0, til...  68.6 us
    all_to_all x1, waiting for transfers between devices, local(): lax.all_to_all(spread, 'mp', split_axis=1, concat_axis=1, tiled=True)  31.1 us
    dot_general x4, matrix products, local(): jnp.einsum('wqk,wkd->wqd', weights, own_values, preferred_element_type=jn...  26 us
    dot_general x1, matrix products, local(): projected = jnp.dot(normed, fused, preferred_element_type=jnp.float32)  23.8 us
    all_to_all x1, starting transfers between devices, local(): lax.all_to_all(jnp.stack([fused_rows] * lax.axis_size('seq')), 'seq', 0, 0)  13.4 us
    all_to_all x1, starting transfers between devices, local(): lax.all_to_all(sectioned, ('seq', 'mp'), split_axis=0, concat_axis=0, til...  11.7 us
    convert_element_type x1, other arithmetic, local(): turned.astype(jnp.bfloat16).reshape(windows, window_tokens, 2 * width)  10.4 us
  transfers between devices with their start and end apart: 4, of which 3 were waited for; matrix products, arithmetic and copies ran while one was open for 26% of the time, Pallas kernels for 0%

profile of v1, /device:TPU:1, one launch (start us, length us, event | category | flops | bytes accessed | tf_op | source)
XLA Modules:
  0.0 419.1 jit_solution(13290080205929699210)
XLA Ops:
  9.6 3.0 stack.2
  12.6 13.4 %all-to-all-start = ((bf16[64,20,1920]{2,1,0:T(8,128)(2,1)}), bf16[64,20,1920]{2,1,0:T(8,128)(2,1)}, u32[]{:S(2)}, u32[]{:S(2)}) async-start(bf16[64,20,1920]{2,1,0:T(8,128)(2,1)} %stack.2), calls=%async_computation | async-start | bytes 11796480 | tf_op jit(solution)/shard_map/all_to_all | solution.py:97
  27.0 6.1 %fusion.4 = f32[4096]{0:T(1024)S(1)} fusion(bf16[4096,1280]{1,0:T(8,128)(2,1)} %param.6), kind=kLoop, calls=%fused_computation.7 | loop fusion | flops 15724544 | bytes 10502144 | tf_op jit(solution)/shard_map/reduce_sum | solution.py:60
  33.3 4.8 %fusion.69 = (f32[4096,80]{0,1:T(8,128)S(1)}, f32[4096,80]{0,1:T(8,128)S(1)}) fusion(f32[4096,20]{0,1:T(8,128)S(1)} %get-tuple-element.19, f32[4096,20]{0,1:T(8,128)S(1)} %get-tuple-element.18), kind=kLoop, calls=%fused_computation.88 | loop fusion | flops 983040 | bytes 3276800 | tf_op jit(solution)/shard_map/cos | solution.py:23
  38.0 118.5 %all-to-all-done = bf16[64,20,1920]{2,1,0:T(8,128)(2,1)} async-done(((bf16[64,20,1920]{2,1,0:T(8,128)(2,1)}), bf16[64,20,1920]{2,1,0:T(8,128)(2,1)}, u32[]{:S(2)}, u32[]{:S(2)}) %all-to-all-start) | async-done | bytes 4915232 | tf_op jit(solution)/shard_map/all_to_all | solution.py:97
  156.5 7.5 %reshape.649 = bf16[1280,1920]{1,0:T(8,128)(2,1)} reshape(bf16[64,20,1920]{2,1,0:T(8,128)(2,1)} %all-to-all-done) | data formatting | bytes 9830400 | tf_op jit(solution)/shard_map/reshape | solution.py:96
  164.1 2.6 slice.72
  166.7 2.2 copy.67
  168.9 23.8 %fusion.6 = f32[4096,1600]{0,1:T(8,128)} fusion(bf16[4096,1280]{1,0:T(8,128)(2,1)} %param.6, f32[4096]{0:T(1024)S(1)} %add_rsqrt_fusion, bf16[1280,1920]{1,0:T(8,128)(2,1)} %reshape.649), kind=kOutput, calls=%fused_computation.9 | convolution fusion | flops 16792944640 | bytes 40976384 | tf_op jit(solution)/shard_map/dot_general | solution.py:110
  192.8 4.4 %slice.125 = bf16[4096,320]{0,1:T(8,128)(2,1)} slice(f32[4096,1600]{0,1:T(8,128)} %fusion.6), slice={[0:4096], [1280:1600]} | slice | bytes 5242880 | tf_op jit(solution)/shard_map/slice | solution.py:116
  197.2 10.4 %fusion.9 = bf16[4096,640]{0,1:T(8,128)(2,1)} fusion(f32[4096,1600]{0,1:T(8,128)} %fusion.6, f32[4096,80]{0,1:T(8,128)S(1)} %get-tuple-element.11, f32[4096,80]{0,1:T(8,128)S(1)} %get-tuple-element.10), kind=kLoop, calls=%fused_computation.12 | loop fusion | flops 10485760 | bytes 28835840 | tf_op jit(solution)/shard_map/convert_element_type | solution.py:113
  207.6 7.9 %copy.60 = bf16[4096,640]{1,0:T(8,128)(2,1)} copy(bf16[4096,640]{0,1:T(8,128)(2,1)} %fusion.9) | data formatting | bytes 10485760 | tf_op jit(solution)/shard_map/convert_element_type | solution.py:113
  215.5 3.5 copy.61
  219.1 5.4 %fusion.20 = f32[64,64,64]{1,2,0:T(8,128)S(1)} fusion(pred[320]{0:T(512)(128)(4,1)S(1)} %broadcast_compare_fusion.1, bf16[64,64,640]{2,1,0:T(8,128)(2,1)} %bitcast.53), kind=kOutput, calls=%fused_computation.28 | convolution fusion | flops 169082880 | bytes 7340352 | tf_op jit(solution)/shard_map/wqd,wkd->wqk/dot_general | solution.py:124
  227.2 1.4 fusion.28
  228.6 1.4 fusion.24
  231.9 5.4 %fusion.22 = f32[64,64,320]{2,1,0:T(8,128)} fusion(bf16[64,64,320]{2,1,0:T(8,128)(2,1)S(1)} %bitcast.49, pred[320]{0:T(512)(128)(4,1)S(1)} %broadcast_compare_fusion.3, f32[64,64]{1,0:T(8,128)S(1)} %fusion.127, f32[64,64,64]{1,2,0:T(8,128)} %copy-done.8), kind=kOutput, calls=%fused_computation.30 | convolution fusion | flops 170135616 | bytes 8929600 | tf_op jit(solution)/shard_map/wqk,wkd->wqd/dot_general | solution.py:131
  237.3 5.4 %fusion.14 = f32[64,64,320]{2,1,0:T(8,128)} fusion(bf16[64,64,320]{2,1,0:T(8,128)(2,1)S(1)} %bitcast.50, pred[320]{0:T(512)(128)(4,1)S(1)} %broadcast_compare_fusion, f32[64,64]{1,0:T(8,128)S(1)} %fusion.125, f32[64,64,64]{1,2,0:T(8,128)} %copy-done.7), kind=kOutput, calls=%fused_computation.22 | convolution fusion | flops 170135616 | bytes 8929600 | tf_op jit(solution)/shard_map/wqk,wkd->wqd/dot_general | solution.py:131
  242.7 5.3 %fusion.18 = f32[64,64,320]{2,1,0:T(8,128)} fusion(bf16[64,64,320]{2,1,0:T(8,128)(2,1)S(1)} %bitcast.51, pred[320]{0:T(512)(128)(4,1)S(1)} %broadcast_compare_fusion.1, f32[64,64]{1,0:T(8,128)S(1)} %fusion.126, f32[64,64,64]{1,2,0:T(8,128)} %copy-done.6), kind=kOutput, calls=%fused_computation.26 | convolution fusion | flops 170135616 | bytes 8929600 | tf_op jit(solution)/shard_map/wqk,wkd->wqd/dot_general | solution.py:131
  248.0 9.9 %add_convert_fusion = bf16[64,64,320]{2,1,0:T(8,128)(2,1)S(1)} fusion(f32[64,64,320]{2,1,0:T(8,128)} %fusion.14, f32[64,64,320]{2,1,0:T(8,128)} %fusion.18, f32[64,64,320]{2,1,0:T(8,128)} %fusion.22, bf16[64,64,320]{2,1,0:T(8,128)(2,1)} %bitcast.52, pred[320]{0:T(512)(128)(4,1)S(1)} %broadcast_compare_fusion.2, f32[64,64]{1,0:T(8,128)S(1)} %fusion.128, ...), kind=kOutput, calls=%fused_computation.15 | convolution fusion | flops 175378496 | bytes 22036800 | tf_op jit(solution)/shard_map/wqk,wkd->wqd/dot_general | solution.py:131
  258.0 2.0 copy.66
  259.9 3.9 all-to-all-start.1
  263.9 3.4 constant_dynamic-slice_fusion
  267.3 31.1 %all-to-all-done.1 = bf16[64,4,16,320]{3,2,0,1:T(8,128)(2,1)S(1)} async-done(((bf16[64,4,16,320]{3,2,0,1:T(8,128)(2,1)}), bf16[64,4,16,320]{3,2,0,1:T(8,128)(2,1)S(1)}, u32[]{:S(2)}, u32[]{:S(2)}) %all-to-all-start.1) | async-done | bytes 2621472 | tf_op jit(solution)/shard_map/all_to_all | solution.py:136
  298.4 7.3 %fusion.11 = bf16[1024,1280]{1,0:T(8,128)(2,1)} fusion(bf16[1024,1280]{1,0:T(8,128)(2,1)} %bitcast.58, bf16[1024,4,320]{2,0,1:T(8,128)(2,1)S(1)} %bitcast.57, bf16[1280,4,320]{0,2,1:T(8,128)(2,1)} %bitcast.61), kind=kOutput, calls=%fused_computation.18 | convolution fusion | flops 3359375360 | bytes 11141120 | tf_op jit(solution)/shard_map/dot_general | solution.py:138
  305.7 6.1 %reshape.654 = bf16[64,16,4,320]{3,2,1,0:T(4,128)(2,1)S(1)} reshape(bf16[1024,1280]{1,0:T(8,128)(2,1)} %fusion.11) | data formatting | bytes 5242880 | tf_op jit(solution)/shard_map/reshape | solution.py:147
  311.8 2.4 copy.69
  314.2 11.7 %all-to-all-start.2 = ((bf16[256,16,320]{2,1,0:T(8,128)(2,1)}), bf16[256,16,320]{2,1,0:T(8,128)(2,1)S(1)}, u32[]{:S(2)}, u32[]{:S(2)}) async-start(bf16[256,16,320]{2,1,0:T(8,128)(2,1)} %bitcast.47), calls=%async_computation.2 | async-start | bytes 6291456 | tf_op jit(solution)/shard_map/all_to_all | solution.py:151
  333.2 68.6 %all-to-all-done.2 = bf16[256,16,320]{2,1,0:T(8,128)(2,1)S(1)} async-done(((bf16[256,16,320]{2,1,0:T(8,128)(2,1)}), bf16[256,16,320]{2,1,0:T(8,128)(2,1)S(1)}, u32[]{:S(2)}, u32[]{:S(2)}) %all-to-all-start.2) | async-done | bytes 2621472 | tf_op jit(solution)/shard_map/all_to_all | solution.py:151
  401.8 2.7 gather_fusion
  404.5 5.0 %fusion.13 = bf16[4096,320]{1,0:T(8,128)(2,1)S(1)} fusion(bf16[256,16,320]{2,1,0:T(8,128)(2,1)} %gather_fusion, pred[4096]{0:T(1024)(128)(4,1)S(1)} %broadcast_in_dim.141, pred[4096]{0:T(1024)(128)(4,1)S(1)} %broadcast_in_dim.135), kind=kLoop, calls=%fused_computation.21 | loop fusion | flops 2621440 | bytes 5251072 | tf_op jit(solution)/shard_map/vmap(jit(_where))/select_n | solution.py:163
  409.6 2.7 copy.70
  (68 shorter events, 10.9 us)
Async XLA Ops:
  12.6 13.7 %copy-start.3 = (s32[64,64]{1,0:T(8,128)S(1)}, s32[64,64]{1,0:T(8,128)}, u32[]{:S(2)}) copy-start(s32[64,64]{1,0:T(8,128)} %param.11) | copy-start | bytes 49156
  12.6 13.8 %copy-start.4 = (s32[64]{0:T(128)S(1)}, s32[64]{0:T(128)}, u32[]{:S(2)}) copy-start(s32[64]{0:T(128)} %param.10) | copy-start | bytes 772
  12.6 144.0 %all-to-all-start = ((bf16[64,20,1920]{2,1,0:T(8,128)(2,1)}), bf16[64,20,1920]{2,1,0:T(8,128)(2,1)}, u32[]{:S(2)}, u32[]{:S(2)}) async-start(bf16[64,20,1920]{2,1,0:T(8,128)(2,1)} %stack.2), calls=%async_computation | async-start | bytes 11796480 | tf_op jit(solution)/shard_map/all_to_all | solution.py:97
  26.0 272.4 %all-gather.2.cloned.1.call-start = ((), (), s32[]{:S(2)}) async-start(), calls=%async_computation.3 | async-start | bytes 4096000 | tf_op jit(solution)/shard_map/all_gather | solution.py:101
  219.1 23.6 %copy-start = (bf16[4096,320]{1,0:T(8,128)(2,1)}, bf16[4096,320]{1,0:T(8,128)(2,1)S(1)}, u32[]{:S(2)}) copy-start(bf16[4096,320]{1,0:T(8,128)(2,1)S(1)} %copy.61) | copy-start | bytes 7864324
  219.1 6.7 %copy-start.1 = (bf16[4096,640]{1,0:T(8,128)(2,1)S(1)}, bf16[4096,640]{1,0:T(8,128)(2,1)}, u32[]{:S(2)}) copy-start(bf16[4096,640]{1,0:T(8,128)(2,1)} %copy.60) | copy-start | bytes 15728644
  224.4 1.4 copy-start.6
  227.2 2.8 copy-start.7
  228.6 2.7 copy-start.2
  230.0 2.0 copy-start.8
  259.9 38.5 %all-to-all-start.1 = ((bf16[64,4,16,320]{3,2,0,1:T(8,128)(2,1)}), bf16[64,4,16,320]{3,2,0,1:T(8,128)(2,1)S(1)}, u32[]{:S(2)}, u32[]{:S(2)}) async-start(bf16[64,4,16,320]{3,2,0,1:T(8,128)(2,1)} %copy.66), calls=%async_computation.1 | async-start | bytes 6291456 | tf_op jit(solution)/shard_map/all_to_all | solution.py:136
  314.2 14.9 %copy-start.5 = (s32[64]{0:T(128)S(1)}, s32[64]{0:T(128)}, u32[]{:S(2)}) copy-start(s32[64]{0:T(128)} %param.9) | copy-start | bytes 772
  314.2 87.6 %all-to-all-start.2 = ((bf16[256,16,320]{2,1,0:T(8,128)(2,1)}), bf16[256,16,320]{2,1,0:T(8,128)(2,1)S(1)}, u32[]{:S(2)}, u32[]{:S(2)}) async-start(bf16[256,16,320]{2,1,0:T(8,128)(2,1)} %bitcast.47), calls=%async_computation.2 | async-start | bytes 6291456 | tf_op jit(solution)/shard_map/all_to_all | solution.py:151
Sparse Core Ops, SparseCore 0:
  169.0 41.2 all-gather.1
